TPU v7x, 256 devices: a whole 4x4x8 slice. The times are simulated.
256 devices in a mesh: dp: 8 (over y, core), expert: 32 (over z, x).
Axes of the slice: x: 4, y: 4, z: 8, core: 2. Of those that a mesh axis runs over, the one named last changes fastest.
Arguments:
- tokens: bfloat16 [4096, 4096], P('expert', 'dp'), may hold values from -6 to 6
- expert_ids: int32 [4096, 8], P('expert'), may hold values from 0 to 63, all different within a row; in each aligned block of 128 rows (0 to 127, 128 to 255, ...) at most 24 rows name the same one
- route_weights: float32 [4096, 8], P('expert'), may hold values from 0.1 to 0.4
- gate_up_weight: bfloat16 [64, 4096, 1536], P('expert', 'dp'), may hold values from -0.09375 to 0.09375
- down_weight: bfloat16 [64, 768, 4096], P('expert', None, 'dp'), may hold values from -0.21875 to 0.21875
- out_grad: bfloat16 [4096, 4096], P('expert', 'dp'), may hold values from -6 to 6
Outputs:
- layer_out: bfloat16 [4096, 4096], P('expert', 'dp')
- token_grad: bfloat16 [4096, 4096], P('expert', 'dp')
- route_grad: float32 [4096, 8], P('expert')
- gate_up_grad: bfloat16 [64, 4096, 1536], P('expert', 'dp')
- down_grad: bfloat16 [64, 768, 4096], P('expert', None, 'dp')
Inputs may be any that keep to these rules, and one draw needn't show every extreme that they name: `expert_ids`: each row names 8 different experts. Among the 128 rows of one group no expert is named more than 24 times, and in every draw some group names some expert exactly 24 times.
All inputs are finite; a program needn't handle non-finite values.
Results may differ from a plain program's by a relative error of at most 0.029.
Values may be sent and summed in bfloat16 or wider, within the bound.
No kernel may reach another device: no remote copies, remote signals or barrier semaphores. Data moves between devices by JAX's collectives and lax.ppermute only.
A program may use at most 128 MiB of HBM per device.

v0:
```python
import jax
import jax.numpy as jnp
from jax import lax
from jax.sharding import PartitionSpec as P


def local(tokens, expert_ids, route_weights, gate_up_weight, down_weight, out_grad):
    tok_count, piece_width = tokens.shape
    top_count = expert_ids.shape[1]
    group_count = lax.axis_size("expert")
    local_count = gate_up_weight.shape[0]
    hidden_units = down_weight.shape[1]
    expert_total = local_count * group_count
    capacity = 3 * tok_count * top_count // (2 * expert_total)
    slot_count = expert_total * capacity
    rows_all = group_count * capacity
    route_count = tok_count * top_count
    block_shape = (local_count, group_count, capacity, piece_width)
    route_ids = expert_ids.reshape(-1)
    onehot = (route_ids[:, None] == jnp.arange(expert_total, dtype=jnp.int32)[None, :]).astype(
        jnp.bfloat16
    )
    order = jnp.arange(route_count, dtype=jnp.int32)
    lower = (order[None, :] < order[:, None]).astype(jnp.bfloat16)
    earlier = jnp.dot(lower, onehot, preferred_element_type=jnp.float32)
    slot_rank = jnp.sum(onehot.astype(jnp.float32) * earlier, axis=1).astype(jnp.int32)
    slot_index = (
        route_ids % local_count * rows_all + route_ids // local_count * capacity + slot_rank
    )
    route_hit = slot_index[:, None] == jnp.arange(slot_count, dtype=jnp.int32)[None, :]
    token_hit = jnp.any(route_hit.reshape(tok_count, top_count, slot_count), axis=1).astype(
        jnp.bfloat16
    )
    weight_flat = route_weights.reshape(-1)
    slot_weight = jnp.sum(jnp.where(route_hit, weight_flat[:, None], 0.0), axis=0)
    outbound = lax.dot_general(
        token_hit, tokens, (((0,), (0,)), ((), ())), preferred_element_type=jnp.float32
    ).astype(jnp.bfloat16)
    grad_outbound = (
        slot_weight[:, None]
        * lax.dot_general(
            token_hit, out_grad, (((0,), (0,)), ((), ())), preferred_element_type=jnp.float32
        )
    ).astype(jnp.bfloat16)
    both = jnp.stack([outbound, grad_outbound]).reshape((2,) + block_shape)
    both = lax.all_to_all(both, "expert", split_axis=2, concat_axis=2, tiled=True)
    arrived = both[0].reshape(local_count, rows_all, piece_width)
    grad_arrived = both[1].reshape(local_count, rows_all, piece_width)
    gate_up_part = jnp.einsum(
        "lrk,lkf->rlf", arrived, gate_up_weight, preferred_element_type=jnp.float32
    ).astype(jnp.bfloat16)
    hidden_grad_part = jnp.einsum(
        "lrk,lfk->rlf", grad_arrived, down_weight, preferred_element_type=jnp.float32
    ).astype(jnp.bfloat16)
    summed = lax.psum_scatter(
        jnp.concatenate([gate_up_part, hidden_grad_part], axis=2),
        "dp",
        scatter_dimension=0,
        tiled=True,
    ).astype(jnp.float32)
    gate_pre = summed[..., :hidden_units]
    up_pre = summed[..., hidden_units : 2 * hidden_units]
    hidden_grad = summed[..., 2 * hidden_units :]
    sigmoid_gate = jax.nn.sigmoid(gate_pre)
    activation = gate_pre * sigmoid_gate
    hidden_mine = (activation * up_pre).astype(jnp.bfloat16)
    gate_grad = hidden_grad * up_pre * sigmoid_gate * (1.0 + gate_pre * (1.0 - sigmoid_gate))
    up_grad = hidden_grad * activation
    preact_grad = jnp.concatenate([gate_grad, up_grad], axis=2).astype(jnp.bfloat16)
    hidden_all = lax.all_gather(hidden_mine, "dp", axis=0, tiled=True)
    preact_grad_all = lax.all_gather(preact_grad, "dp", axis=0, tiled=True)
    out_slice = jnp.einsum(
        "rlf,lfk->lrk", hidden_all, down_weight, preferred_element_type=jnp.float32
    ).astype(jnp.bfloat16)
    grad_routes = jnp.repeat(out_grad, top_count, axis=0).astype(jnp.float32)
    returned = lax.all_to_all(
        out_slice.reshape(block_shape), "expert", split_axis=1, concat_axis=1, tiled=True
    )
    route_pick = route_hit.astype(jnp.bfloat16)
    y_routes = jnp.dot(
        route_pick, returned.reshape(slot_count, piece_width), preferred_element_type=jnp.float32
    )
    layer_out = (
        (weight_flat[:, None] * y_routes)
        .reshape(tok_count, top_count, piece_width)
        .sum(axis=1)
        .astype(jnp.bfloat16)
    )
    partial_dot = jnp.sum(grad_routes * y_routes, axis=1).reshape(tok_count, top_count)
    route_grad = lax.psum(partial_dot, "dp")
    x_grad_slice = jnp.einsum(
        "rlf,lkf->lrk", preact_grad_all, gate_up_weight, preferred_element_type=jnp.float32
    ).astype(jnp.bfloat16)
    gate_up_grad = jnp.einsum(
        "lrk,rlf->lkf", arrived, preact_grad_all, preferred_element_type=jnp.float32
    ).astype(jnp.bfloat16)
    down_grad = jnp.einsum(
        "rlf,lrk->lfk", hidden_all, grad_arrived, preferred_element_type=jnp.float32
    ).astype(jnp.bfloat16)
    grad_back = lax.all_to_all(
        x_grad_slice.reshape(block_shape), "expert", split_axis=1, concat_axis=1, tiled=True
    )
    token_grad = jnp.dot(
        token_hit, grad_back.reshape(slot_count, piece_width), preferred_element_type=jnp.float32
    ).astype(jnp.bfloat16)
    return (layer_out, token_grad, route_grad, gate_up_grad, down_grad)


def solution(mesh):
    placed = (
        P("expert", "dp"),
        P("expert", None),
        P("expert", None),
        P("expert", "dp", None),
        P("expert", None, "dp"),
        P("expert", "dp"),
    )
    return jax.shard_map(
        local,
        mesh=mesh,
        in_specs=placed,
        out_specs=(
            P("expert", "dp"),
            P("expert", "dp"),
            P("expert", None),
            P("expert", "dp", None),
            P("expert", None, "dp"),
        ),
        check_vma=False,
    )
```

profile of v0, /device:TPU:4, one launch (start us, length us, event | category | flops | bytes accessed | tf_op | source)
XLA Modules:
  0.0 303.9 jit_solution(3204589052721626172)
XLA Ops:
  9.9 3.2 %fusion.1 = pred[128,1536]{1,0:T(8,128)(4,1)S(1)} fusion(s32[128,8]{1,0:T(8,128)S(1)} %fusion.13), kind=kLoop, calls=%fused_computation.5 | loop fusion | flops 2949120 | bytes 200704 | tf_op jit(solution)/shard_map/reduce_or | solution.py:31
  13.9 1.5 convolution_convert_fusion.1
  16.9 84.4 %all_to_all.15 = bf16[2,2,32,24,512]{4,3,1,0,2:T(8,128)(2,1)S(1)} all-to-all(bf16[2,2,32,24,512]{4,3,1,0,2:T(8,128)(2,1)S(1)} %copy.74), channel_id=1, replica_groups=mesh['dp'=8,'expert'=32] {'expert'}, dimensions={2} | all-to-all | bytes 6291456 | tf_op jit(solution)/shard_map/all_to_all | solution.py:46
  101.8 4.2 %convert_bitcast_fusion = bf16[768,2,1536]{2,0,1:T(8,128)(2,1)} fusion(bf16[2,768,512]{2,1,0:T(8,128)(2,1)S(1)} %bitcast.40, bf16[2,512,1536]{2,1,0:T(8,128)(2,1)S(1)} %copy-done), kind=kOutput, calls=%fused_computation.6 | convolution fusion | flops 2418278400 | bytes 9437184 | tf_op jit(solution)/shard_map/lrk,lkf->rlf/dot_general | solution.py:49
  106.0 2.8 convert_bitcast_fusion.1
  108.9 6.4 %pad_maximum_fusion = bf16[768,2,2304]{2,0,1:T(8,128)(2,1)} fusion(bf16[768,2,768]{2,0,1:T(8,128)(2,1)} %convert_bitcast_fusion.1, bf16[768,2,1536]{2,0,1:T(8,128)(2,1)} %convert_bitcast_fusion), kind=kLoop, calls=%fused_computation | loop fusion | flops 14155776 | bytes 14155776 | tf_op jit(solution)/shard_map/concatenate | solution.py:56
  115.4 45.8 %reduce-scatter.2.cloned.1.call-done = bf16[96,2,2304]{2,0,1:T(8,128)(2,1)} async-done(((bf16[768,2,2304]{2,0,1:T(8,128)(2,1)}), bf16[96,2,2304]{2,0,1:T(8,128)(2,1)}) %reduce-scatter.2.cloned.1.call-update) | async-done | bytes 884752 | tf_op jit(solution)/shard_map/reduce_scatter | solution.py:55
  161.2 1.3 convert_element_type.80
  163.7 1.9 pad_maximum_fusion.2
  165.6 26.0 %all-gather.3.cloned.1.call-done = bf16[768,2,768]{2,0,1:T(8,128)(2,1)} async-done(((bf16[96,2,768]{2,0,1:T(8,128)(2,1)}), bf16[768,2,768]{2,0,1:T(8,128)(2,1)}) %all-gather.3.cloned.1.call-update) | async-done | bytes 2359312 | tf_op jit(solution)/shard_map/all_gather | solution.py:70
  191.6 3.5 %convolution_convert_fusion.3 = bf16[2,768,512]{2,1,0:T(8,128)(2,1)S(1)} fusion(bf16[768,2,768]{2,0,1:T(8,128)(2,1)} %all-gather.3.cloned.1.call-done, bf16[2,768,512]{2,1,0:T(8,128)(2,1)} %param.10), kind=kOutput, calls=%fused_computation.20 | convolution fusion | flops 1208745984 | bytes 5505024 | tf_op jit(solution)/shard_map/rlf,lfk->lrk/dot_general | solution.py:72
  195.1 1.4 copy.66
  196.5 10.2 %all-to-all-start.1 = ((bf16[2,32,24,512]{3,2,0,1:T(8,128)(2,1)}), bf16[2,32,24,512]{3,2,0,1:T(8,128)(2,1)}, u32[]{:S(2)}, u32[]{:S(2)}) async-start(bf16[2,32,24,512]{3,2,0,1:T(8,128)(2,1)} %copy.66), calls=%async_computation.2 | async-start | bytes 3145728 | tf_op jit(solution)/shard_map/all_to_all | solution.py:76
  206.7 24.8 %all-gather.5.cloned.1.call-done = bf16[768,2,1536]{2,0,1:T(8,128)(2,1)} async-done(((bf16[96,2,1536]{2,0,1:T(8,128)(2,1)}), bf16[768,2,1536]{2,0,1:T(8,128)(2,1)}) %all-gather.5.cloned.1.call-update) | async-done | bytes 4718608 | tf_op jit(solution)/shard_map/all_gather | solution.py:71
  231.4 5.0 %convolution_convert_fusion.4 = bf16[2,768,512]{2,1,0:T(8,128)(2,1)S(1)} fusion(bf16[768,2,1536]{2,0,1:T(8,128)(2,1)} %all-gather.5.cloned.1.call-done, bf16[2,512,1536]{2,1,0:T(8,128)(2,1)S(1)} %copy-done), kind=kOutput, calls=%fused_computation.21 | convolution fusion | flops 2416705536 | bytes 9437184 | tf_op jit(solution)/shard_map/rlf,lkf->lrk/dot_general | solution.py:91
  236.4 1.4 copy.68
  237.8 8.6 %all-to-all-done.1 = bf16[2,32,24,512]{3,2,0,1:T(8,128)(2,1)} async-done(((bf16[2,32,24,512]{3,2,0,1:T(8,128)(2,1)}), bf16[2,32,24,512]{3,2,0,1:T(8,128)(2,1)}, u32[]{:S(2)}, u32[]{:S(2)}) %all-to-all-start.1) | async-done | bytes 1572896 | tf_op jit(solution)/shard_map/all_to_all | solution.py:76
  246.4 5.6 %all-to-all-start.2 = ((bf16[2,32,24,512]{3,2,0,1:T(8,128)(2,1)}), bf16[2,32,24,512]{3,2,0,1:T(8,128)(2,1)}, u32[]{:S(2)}, u32[]{:S(2)}) async-start(bf16[2,32,24,512]{3,2,0,1:T(8,128)(2,1)} %copy.68), calls=%async_computation.3 | async-start | bytes 3145728 | tf_op jit(solution)/shard_map/all_to_all | solution.py:100
  252.0 4.7 %convolution_convert_fusion.2 = bf16[2,768,512]{2,1,0:T(8,128)(2,1)} fusion(bf16[768,2,768]{2,0,1:T(8,128)(2,1)} %all-gather.3.cloned.1.call-done, bf16[2,768,512]{2,1,0:T(8,128)(2,1)} %bitcast.43), kind=kOutput, calls=%fused_computation.19 | convolution fusion | flops 1208745984 | bytes 5505024 | tf_op jit(solution)/shard_map/rlf,lrk->lfk/dot_general | solution.py:97
  256.7 1.5 copy.67
  258.3 2.9 bitcast_reduce_fusion
  261.5 25.5 %psum.7 = f32[128,8]{1,0:T(8,128)S(1)} all-reduce(f32[128,8]{1,0:T(8,128)S(1)} %reshape.113), channel_id=1, replica_groups=mesh['dp'=8,'expert'=32] {'dp'}, use_global_device_ids=true, to_apply=%region_6.7 | all-reduce | flops 1024 | bytes 8192 | tf_op jit(solution)/shard_map/psum | solution.py:90
  287.7 7.1 %convolution_convert_fusion = bf16[2,512,1536]{2,1,0:T(8,128)(2,1)} fusion(bf16[2,768,512]{2,1,0:T(8,128)(2,1)} %bitcast.41, bf16[768,2,1536]{2,0,1:T(8,128)(2,1)} %all-gather.5.cloned.1.call-done), kind=kOutput, calls=%fused_computation.9 | convolution fusion | flops 2417491968 | bytes 9437184 | tf_op jit(solution)/shard_map/lrk,rlf->lkf/dot_general | solution.py:94
  294.8 1.5 copy.69
  (39 shorter events, 8.8 us)
Async XLA Ops:
  7.2 94.6 %copy-start = (bf16[2,512,1536]{2,1,0:T(8,128)(2,1)S(1)}, bf16[2,512,1536]{2,1,0:T(8,128)(2,1)}, u32[]{:S(2)}) copy-start(bf16[2,512,1536]{2,1,0:T(8,128)(2,1)} %param.9) | copy-start | bytes 9437188
  7.2 154.0 %reduce-scatter.2.cloned.1.call-start = ((), (), s32[]{:S(2)}) async-start(), calls=%async_computation.4 | async-start | bytes 7962624 | tf_op jit(solution)/shard_map/reduce_scatter | solution.py:55
  8.3 7.2 %copy-start.3 = (bf16[128,512]{1,0:T(8,128)(2,1)S(1)}, bf16[128,512]{1,0:T(8,128)(2,1)}, u32[]{:S(2)}) copy-start(bf16[128,512]{1,0:T(8,128)(2,1)} %param.11) | copy-start | bytes 393220
  101.7 4.4 %copy-start.1 = (bf16[1,2,32,24,512]{4,3,2,1,0:T(8,128)(2,1)}, bf16[1,2,32,24,512]{4,3,2,1,0:T(8,128)(2,1)S(1)}, u32[]{:S(2)}) copy-start(bf16[1,2,32,24,512]{4,3,2,1,0:T(8,128)(2,1)S(1)} %copy.63) | copy-start | bytes 4718596
  101.8 4.2 %copy-start.2 = (bf16[1,2,32,24,512]{4,3,2,1,0:T(8,128)(2,1)}, bf16[1,2,32,24,512]{4,3,2,1,0:T(8,128)(2,1)S(1)}, u32[]{:S(2)}) copy-start(bf16[1,2,32,24,512]{4,3,2,1,0:T(8,128)(2,1)S(1)} %copy.64) | copy-start | bytes 4718596
  101.8 4.2 %copy-start.4 = (bf16[2,768,512]{2,1,0:T(8,128)(2,1)S(1)}, bf16[2,768,512]{2,1,0:T(8,128)(2,1)}, u32[]{:S(2)}) copy-start(bf16[2,768,512]{2,1,0:T(8,128)(2,1)} %param.10) | copy-start | bytes 4718596
  115.3 76.3 %all-gather.3.cloned.1.call-start = ((), (), s32[]{:S(2)}) async-start(), calls=%async_computation.5 | async-start | bytes 2654208 | tf_op jit(solution)/shard_map/all_gather | solution.py:70
  163.7 67.8 %all-gather.5.cloned.1.call-start = ((), (), s32[]{:S(2)}) async-start(), calls=%async_computation.6 | async-start | bytes 5308416 | tf_op jit(solution)/shard_map/all_gather | solution.py:71
  196.5 49.9 %all-to-all-start.1 = ((bf16[2,32,24,512]{3,2,0,1:T(8,128)(2,1)}), bf16[2,32,24,512]{3,2,0,1:T(8,128)(2,1)}, u32[]{:S(2)}, u32[]{:S(2)}) async-start(bf16[2,32,24,512]{3,2,0,1:T(8,128)(2,1)} %copy.66), calls=%async_computation.2 | async-start | bytes 3145728 | tf_op jit(solution)/shard_map/all_to_all | solution.py:76
  246.4 48.4 %all-to-all-start.2 = ((bf16[2,32,24,512]{3,2,0,1:T(8,128)(2,1)}), bf16[2,32,24,512]{3,2,0,1:T(8,128)(2,1)}, u32[]{:S(2)}, u32[]{:S(2)}) async-start(bf16[2,32,24,512]{3,2,0,1:T(8,128)(2,1)} %copy.68), calls=%async_computation.3 | async-start | bytes 3145728 | tf_op jit(solution)/shard_map/all_to_all | solution.py:100
Sparse Core Ops, SparseCore 0:
  115.4 45.7 reduce-scatter.1
  163.8 27.7 all-gather.2
  194.0 37.3 all-gather.4
where the time goes:
time: 304 us
  blocking collectives  110 us (36%)
  waiting for transfers between devices  105 us (35%)
  matrix products  34 us (11%)
  starting transfers between devices  15.9 us (5%)
  other arithmetic  15.4 us (5%)
  between operations  14 us (5%)
  local copies, waits for them, and re-layouts  9.53 us (3%)
    all_to_all x1, blocking collectives, local(): lax.all_to_all(both, 'expert', split_axis=2, concat_axis=2, tiled=True)  84.4 us
    reduce_scatter x1, waiting for transfers between devices, local(): lax.psum_scatter(jnp.concatenate([gate_up_part, hidden_grad_part], axis=2...  45.8 us
    all_gather x1, waiting for transfers between devices, local(): hidden_all = lax.all_gather(hidden_mine, 'dp', axis=0, tiled=True)  26 us
    psum x1, blocking collectives, local(): route_grad = lax.psum(partial_dot, 'dp')  25.5 us
    all_gather x1, waiting for transfers between devices, local(): preact_grad_all = lax.all_gather(preact_grad, 'dp', axis=0, tiled=True)  24.8 us
    all_to_all x1, starting transfers between devices, local(): lax.all_to_all(out_slice.reshape(block_shape), 'expert', split_axis=1, co...  10.2 us
    all_to_all x1, waiting for transfers between devices, local(): lax.all_to_all(out_slice.reshape(block_shape), 'expert', split_axis=1, co...  8.58 us
    dot_general x1, matrix products, local(): jnp.einsum('lrk,rlf->lkf', arrived, preact_grad_all, preferred_element_ty...  7.12 us
  transfers between devices with their start and end apart: 5, of which 4 were waited for; matrix products, arithmetic and copies ran while one was open for 10% of the time, Pallas kernels for 0%

commit v1 on v0

--- a/solution.py
+++ b/solution.py
@@ -68,7 +68,22 @@
     up_grad = hidden_grad * activation
     preact_grad = jnp.concatenate([gate_grad, up_grad], axis=2).astype(jnp.bfloat16)
     hidden_all = lax.all_gather(hidden_mine, "dp", axis=0, tiled=True)
-    preact_grad_all = lax.all_gather(preact_grad, "dp", axis=0, tiled=True)
+    ways, here, step = (lax.axis_size("dp"), lax.axis_index("dp"), preact_grad.shape[0])
+    shape = [n * ways if d == 0 else n for d, n in enumerate(preact_grad.shape)]
+    preact_grad_all = lax.dynamic_update_slice_in_dim(
+        jnp.zeros(shape, preact_grad.dtype), preact_grad, here * step, axis=0
+    )
+    going_up = going_down = preact_grad
+    for far in range(1, ways // 2 + 1):
+        going_up = lax.ppermute(going_up, "dp", [(d, (d + 1) % ways) for d in range(ways)])
+        preact_grad_all = lax.dynamic_update_slice_in_dim(
+            preact_grad_all, going_up, (here - far) % ways * step, axis=0
+        )
+        if 2 * far < ways:
+            going_down = lax.ppermute(going_down, "dp", [(d, (d - 1) % ways) for d in range(ways)])
+            preact_grad_all = lax.dynamic_update_slice_in_dim(
+                preact_grad_all, going_down, (here + far) % ways * step, axis=0
+            )
     out_slice = jnp.einsum(
         "rlf,lfk->lrk", hidden_all, down_weight, preferred_element_type=jnp.float32
     ).astype(jnp.bfloat16)

time: 304 us -> 348 us (1.14)
  waiting for transfers between devices: 105 us -> 124 us
  local copies, waits for them, and re-layouts: 9.53 us -> 19.5 us
  starting transfers between devices: 15.9 us -> 24.8 us
  blocking collectives: 110 us -> 118 us
    ppermute x0 -> x7, waiting for transfers between devices: none -> 31.5 us  [the longest x4 31.3 us: local(): lax.ppermute(going_up, 'dp', [(d, (d + 1) % ways) for d in range(ways)])]
    all_to_all x1, waiting for transfers between devices: 0.01 us -> 26.8 us  [local(): lax.all_to_all(x_grad_slice.reshape(block_shape), 'expert', split_axis=1,...]
    all_gather x1, waiting for transfers between devices: 26 us -> 0.02 us  [local(): hidden_all = lax.all_gather(hidden_mine, 'dp', axis=0, tiled=True)]
    all_gather x1 -> x0, waiting for transfers between devices: 24.8 us -> none  [local(): preact_grad_all = lax.all_gather(preact_grad, 'dp', axis=0, tiled=True)]
    all_to_all x1, waiting for transfers between devices: 8.58 us -> 19.9 us  [local(): lax.all_to_all(out_slice.reshape(block_shape), 'expert', split_axis=1, co...]
    dynamic_update_slice x0 -> x7, local copies, waits for them, and re-layouts: none -> 10.3 us  [the longest x4 5.57 us: local(): lax.dynamic_update_slice_in_dim(preact_grad_all, going_up, (here - far) %...]
    ppermute x0 -> x7, starting transfers between devices: none -> 8.87 us  [the longest x3 8.85 us: local(): lax.ppermute(going_down, 'dp', [(d, (d - 1) % ways) for d in range(ways)])]
    psum x1, blocking collectives: 25.5 us -> 33.9 us  [local(): route_grad = lax.psum(partial_dot, 'dp')]
  transfers between devices with their start and end apart: 5 -> 11, of which waited for: 4 -> 8; matrix products, arithmetic and copies ran while one was open for 10% -> 10% of each run, Pallas kernels for 0% -> 0%
where the time goes in v1:
time: 348 us
  waiting for transfers between devices  124 us (36%)
  blocking collectives  118 us (34%)
  matrix products  32 us (9%)
  starting transfers between devices  24.8 us (7%)
  local copies, waits for them, and re-layouts  19.5 us (6%)
  other arithmetic  15 us (4%)
  between operations  14.3 us (4%)
    all_to_all x1, blocking collectives, local(): lax.all_to_all(both, 'expert', split_axis=2, concat_axis=2, tiled=True)  84.4 us
    reduce_scatter x1, waiting for transfers between devices, local(): lax.psum_scatter(jnp.concatenate([gate_up_part, hidden_grad_part], axis=2...  45.6 us
    psum x1, blocking collectives, local(): route_grad = lax.psum(partial_dot, 'dp')  33.9 us
    ppermute x4, waiting for transfers between devices, local(): lax.ppermute(going_up, 'dp', [(d, (d + 1) % ways) for d in range(ways)])  31.3 us
    all_to_all x1, waiting for transfers between devices, local(): lax.all_to_all(x_grad_slice.reshape(block_shape), 'expert', split_axis=1,...  26.8 us
    all_to_all x1, waiting for transfers between devices, local(): lax.all_to_all(out_slice.reshape(block_shape), 'expert', split_axis=1, co...  19.9 us
    all_to_all x1, starting transfers between devices, local(): lax.all_to_all(x_grad_slice.reshape(block_shape), 'expert', split_axis=1,...  10.1 us
    ppermute x3, starting transfers between devices, local(): lax.ppermute(going_down, 'dp', [(d, (d - 1) % ways) for d in range(ways)])  8.85 us
  transfers between devices with their start and end apart: 11, of which 8 were waited for; matrix products, arithmetic and copies ran while one was open for 10% of the time, Pallas kernels for 0%

profile of v1, /device:TPU:4, one launch (start us, length us, event | category | flops | bytes accessed | tf_op | source)
XLA Modules:
  0.0 347.7 jit_solution(15119195057405333035)
XLA Ops:
  10.0 3.2 fusion.1
  16.9 84.4 %all_to_all.15 = bf16[2,2,32,24,512]{4,3,1,0,2:T(8,128)(2,1)S(1)} all-to-all(bf16[2,2,32,24,512]{4,3,1,0,2:T(8,128)(2,1)S(1)} %copy.74), channel_id=1, replica_groups=mesh['dp'=8,'expert'=32] {'expert'}, dimensions={2} | all-to-all | bytes 6291456 | tf_op jit(solution)/shard_map/all_to_all | solution.py:46
  101.8 4.2 %convert_bitcast_fusion = bf16[768,2,1536]{2,0,1:T(8,128)(2,1)} fusion(bf16[2,768,512]{2,1,0:T(8,128)(2,1)S(1)} %bitcast.40, bf16[2,512,1536]{2,1,0:T(8,128)(2,1)S(1)} %copy-done), kind=kOutput, calls=%fused_computation.6 | convolution fusion | flops 2418278400 | bytes 9437184 | tf_op jit(solution)/shard_map/lrk,lkf->rlf/dot_general | solution.py:49
  106.1 2.8 convert_bitcast_fusion.1
  108.9 6.4 %pad_maximum_fusion = bf16[768,2,2304]{2,0,1:T(8,128)(2,1)} fusion(bf16[768,2,768]{2,0,1:T(8,128)(2,1)} %convert_bitcast_fusion.1, bf16[768,2,1536]{2,0,1:T(8,128)(2,1)} %convert_bitcast_fusion), kind=kLoop, calls=%fused_computation | loop fusion | flops 14155776 | bytes 14155776 | tf_op jit(solution)/shard_map/concatenate | solution.py:56
  115.6 45.6 %reduce-scatter.2.cloned.1.call-done = bf16[96,2,2304]{2,0,1:T(8,128)(2,1)} async-done(((bf16[768,2,2304]{2,0,1:T(8,128)(2,1)}), bf16[96,2,2304]{2,0,1:T(8,128)(2,1)}) %reduce-scatter.2.cloned.1.call-update) | async-done | bytes 884752 | tf_op jit(solution)/shard_map/reduce_scatter | solution.py:55
  163.5 2.4 broadcast_in_dim.26
  166.9 3.0 collective-permute-start.1
  169.9 7.7 %collective-permute-done = bf16[96,2,1536]{2,0,1:T(8,128)(2,1)} collective-permute-done((bf16[96,2,1536]{2,0,1:T(8,128)(2,1)S(1)}, bf16[96,2,1536]{2,0,1:T(8,128)(2,1)}, u32[]{:S(2)}, u32[]{:S(2)}) %collective-permute-start) | collective-permute-done | bytes 589856 | tf_op jit(solution)/shard_map/ppermute | solution.py:78
  177.5 3.0 collective-permute-start.3
  180.5 7.8 %collective-permute-done.2 = bf16[96,2,1536]{2,0,1:T(8,128)(2,1)} collective-permute-done((bf16[96,2,1536]{2,0,1:T(8,128)(2,1)}, bf16[96,2,1536]{2,0,1:T(8,128)(2,1)}, u32[]{:S(2)}, u32[]{:S(2)}) %collective-permute-start.2) | collective-permute-done | bytes 589856 | tf_op jit(solution)/shard_map/ppermute | solution.py:78
  192.2 2.9 collective-permute-start.5
  197.1 9.1 %collective-permute-done.4 = bf16[96,2,1536]{2,0,1:T(8,128)(2,1)S(1)} collective-permute-done((bf16[96,2,1536]{2,0,1:T(8,128)(2,1)}, bf16[96,2,1536]{2,0,1:T(8,128)(2,1)S(1)}, u32[]{:S(2)}, u32[]{:S(2)}) %collective-permute-start.4) | collective-permute-done | bytes 589856 | tf_op jit(solution)/shard_map/ppermute | solution.py:78
  210.1 6.7 %collective-permute-done.6 = bf16[96,2,1536]{2,0,1:T(8,128)(2,1)S(1)} collective-permute-done((bf16[96,2,1536]{2,0,1:T(8,128)(2,1)S(1)}, bf16[96,2,1536]{2,0,1:T(8,128)(2,1)S(1)}, u32[]{:S(2)}, u32[]{:S(2)}) %collective-permute-start.6) | collective-permute-done | bytes 589856 | tf_op jit(solution)/shard_map/ppermute | solution.py:78
  217.6 5.0 %convolution_convert_fusion.4 = bf16[2,768,512]{2,1,0:T(8,128)(2,1)S(1)} fusion(bf16[768,2,1536]{2,0,1:T(8,128)(2,1)} %constant_dynamic-update-slice_fusion, bf16[2,512,1536]{2,1,0:T(8,128)(2,1)S(1)} %copy-done), kind=kOutput, calls=%fused_computation.21 | convolution fusion | flops 2416705536 | bytes 9437184 | tf_op jit(solution)/shard_map/rlf,lkf->lrk/dot_general | solution.py:106
  223.9 10.1 %all-to-all-start.2 = ((bf16[2,32,24,512]{3,2,0,1:T(8,128)(2,1)}), bf16[2,32,24,512]{3,2,0,1:T(8,128)(2,1)S(1)}, u32[]{:S(2)}, u32[]{:S(2)}) async-start(bf16[2,32,24,512]{3,2,0,1:T(8,128)(2,1)} %copy.68), calls=%async_computation.3 | async-start | bytes 3145728 | tf_op jit(solution)/shard_map/all_to_all | solution.py:115
  234.1 3.5 %convolution_convert_fusion.3 = bf16[2,768,512]{2,1,0:T(8,128)(2,1)S(1)} fusion(bf16[768,2,768]{2,0,1:T(8,128)(2,1)} %all-gather.2.cloned.1.call-done, bf16[2,768,512]{2,1,0:T(8,128)(2,1)} %param.10), kind=kOutput, calls=%fused_computation.20 | convolution fusion | flops 1208745984 | bytes 5505024 | tf_op jit(solution)/shard_map/rlf,lfk->lrk/dot_general | solution.py:87
  239.0 26.8 %all-to-all-done.2 = bf16[2,32,24,512]{3,2,0,1:T(8,128)(2,1)S(1)} async-done(((bf16[2,32,24,512]{3,2,0,1:T(8,128)(2,1)}), bf16[2,32,24,512]{3,2,0,1:T(8,128)(2,1)S(1)}, u32[]{:S(2)}, u32[]{:S(2)}) %all-to-all-start.2) | async-done | bytes 1572896 | tf_op jit(solution)/shard_map/all_to_all | solution.py:115
  265.8 5.6 %all-to-all-start.1 = ((bf16[2,32,24,512]{3,2,0,1:T(8,128)(2,1)}), bf16[2,32,24,512]{3,2,0,1:T(8,128)(2,1)S(1)}, u32[]{:S(2)}, u32[]{:S(2)}) async-start(bf16[2,32,24,512]{3,2,0,1:T(8,128)(2,1)} %copy.66), calls=%async_computation.2 | async-start | bytes 3145728 | tf_op jit(solution)/shard_map/all_to_all | solution.py:91
  272.1 7.3 %convolution_convert_fusion = bf16[2,512,1536]{2,1,0:T(8,128)(2,1)} fusion(bf16[2,768,512]{2,1,0:T(8,128)(2,1)} %bitcast.41, bf16[768,2,1536]{2,0,1:T(8,128)(2,1)} %constant_dynamic-update-slice_fusion), kind=kOutput, calls=%fused_computation.9 | convolution fusion | flops 2417491968 | bytes 9437184 | tf_op jit(solution)/shard_map/lrk,rlf->lkf/dot_general | solution.py:109
  279.4 2.6 convolution_convert_fusion.2
  283.1 19.9 %all-to-all-done.1 = bf16[2,32,24,512]{3,2,0,1:T(8,128)(2,1)S(1)} async-done(((bf16[2,32,24,512]{3,2,0,1:T(8,128)(2,1)}), bf16[2,32,24,512]{3,2,0,1:T(8,128)(2,1)S(1)}, u32[]{:S(2)}, u32[]{:S(2)}) %all-to-all-start.1) | async-done | bytes 1572896 | tf_op jit(solution)/shard_map/all_to_all | solution.py:91
  303.1 2.9 bitcast_reduce_fusion
  306.4 33.9 %psum.7 = f32[128,8]{1,0:T(8,128)S(1)} all-reduce(f32[128,8]{1,0:T(8,128)S(1)} %reshape.113), channel_id=1, replica_groups=mesh['dp'=8,'expert'=32] {'dp'}, use_global_device_ids=true, to_apply=%region_6.7 | all-reduce | flops 1024 | bytes 8192 | tf_op jit(solution)/shard_map/psum | solution.py:105
  (66 shorter events, 26.9 us)
Async XLA Ops:
  7.2 94.7 %copy-start = (bf16[2,512,1536]{2,1,0:T(8,128)(2,1)S(1)}, bf16[2,512,1536]{2,1,0:T(8,128)(2,1)}, u32[]{:S(2)}) copy-start(bf16[2,512,1536]{2,1,0:T(8,128)(2,1)} %param.9) | copy-start | bytes 9437188
  7.2 8.3 %copy-start.6 = (bf16[128,512]{1,0:T(8,128)(2,1)S(1)}, bf16[128,512]{1,0:T(8,128)(2,1)}, u32[]{:S(2)}) copy-start(bf16[128,512]{1,0:T(8,128)(2,1)} %param.11) | copy-start | bytes 393220
  7.2 154.0 %reduce-scatter.2.cloned.1.call-start = ((), (), s32[]{:S(2)}) async-start(), calls=%async_computation.4 | async-start | bytes 7962624 | tf_op jit(solution)/shard_map/reduce_scatter | solution.py:55
  101.7 4.4 %copy-start.2 = (bf16[1,2,32,24,512]{4,3,2,1,0:T(8,128)(2,1)}, bf16[1,2,32,24,512]{4,3,2,1,0:T(8,128)(2,1)S(1)}, u32[]{:S(2)}) copy-start(bf16[1,2,32,24,512]{4,3,2,1,0:T(8,128)(2,1)S(1)} %copy.63) | copy-start | bytes 4718596
  101.8 4.2 %copy-start.3 = (bf16[1,2,32,24,512]{4,3,2,1,0:T(8,128)(2,1)}, bf16[1,2,32,24,512]{4,3,2,1,0:T(8,128)(2,1)S(1)}, u32[]{:S(2)}) copy-start(bf16[1,2,32,24,512]{4,3,2,1,0:T(8,128)(2,1)S(1)} %copy.64) | copy-start | bytes 4718596
  101.8 4.2 %copy-start.8 = (bf16[2,768,512]{2,1,0:T(8,128)(2,1)S(1)}, bf16[2,768,512]{2,1,0:T(8,128)(2,1)}, u32[]{:S(2)}) copy-start(bf16[2,768,512]{2,1,0:T(8,128)(2,1)} %param.10) | copy-start | bytes 4718596
  115.3 118.7 %all-gather.2.cloned.1.call-start = ((), (), s32[]{:S(2)}) async-start(), calls=%async_computation.5 | async-start | bytes 2654208 | tf_op jit(solution)/shard_map/all_gather | solution.py:70
  166.9 10.6 %collective-permute-start = (bf16[96,2,1536]{2,0,1:T(8,128)(2,1)S(1)}, bf16[96,2,1536]{2,0,1:T(8,128)(2,1)}, u32[]{:S(2)}, u32[]{:S(2)}) collective-permute-start(bf16[96,2,1536]{2,0,1:T(8,128)(2,1)S(1)} %get-tuple-element.30), channel_id=1, source_target_pairs={{0,32},{32,64},{64,96},{96,128},{128,160},{160,192},{192,224},{224... | collective-permute-start | bytes 1769480 | tf_op jit(solution)/shard_map/ppermute | solution.py:78
  166.9 10.6 %collective-permute-start.1 = (bf16[96,2,1536]{2,0,1:T(8,128)(2,1)S(1)}, bf16[96,2,1536]{2,0,1:T(8,128)(2,1)}, u32[]{:S(2)}, u32[]{:S(2)}) collective-permute-start(bf16[96,2,1536]{2,0,1:T(8,128)(2,1)S(1)} %get-tuple-element.30), channel_id=1, source_target_pairs={{0,224},{32,0},{64,32},{96,64},{128,96},{160,128},{192,160},{224,1... | collective-permute-start | bytes 1769480 | tf_op jit(solution)/shard_map/ppermute | solution.py:83
  177.5 10.8 %collective-permute-start.2 = (bf16[96,2,1536]{2,0,1:T(8,128)(2,1)}, bf16[96,2,1536]{2,0,1:T(8,128)(2,1)}, u32[]{:S(2)}, u32[]{:S(2)}) collective-permute-start(bf16[96,2,1536]{2,0,1:T(8,128)(2,1)} %collective-permute-done), channel_id=1, source_target_pairs={{0,32},{32,64},{64,96},{96,128},{128,160},{160,192},{192,224},{224... | collective-permute-start | bytes 1769480 | tf_op jit(solution)/shard_map/ppermute | solution.py:78
  177.5 14.7 %collective-permute-start.3 = (bf16[96,2,1536]{2,0,1:T(8,128)(2,1)}, bf16[96,2,1536]{2,0,1:T(8,128)(2,1)}, u32[]{:S(2)}, u32[]{:S(2)}) collective-permute-start(bf16[96,2,1536]{2,0,1:T(8,128)(2,1)} %collective-permute-done.1), channel_id=1, source_target_pairs={{0,224},{32,0},{64,32},{96,64},{128,96},{160,128},{192,160},{224,1... | collective-permute-start | bytes 1769480 | tf_op jit(solution)/shard_map/ppermute | solution.py:83
  188.4 17.9 %collective-permute-start.4 = (bf16[96,2,1536]{2,0,1:T(8,128)(2,1)}, bf16[96,2,1536]{2,0,1:T(8,128)(2,1)S(1)}, u32[]{:S(2)}, u32[]{:S(2)}) collective-permute-start(bf16[96,2,1536]{2,0,1:T(8,128)(2,1)} %collective-permute-done.2), channel_id=1, source_target_pairs={{0,32},{32,64},{64,96},{96,128},{128,160},{160,192},{192,224},{224... | collective-permute-start | bytes 1769480 | tf_op jit(solution)/shard_map/ppermute | solution.py:78
  192.2 17.0 %collective-permute-start.5 = (bf16[96,2,1536]{2,0,1:T(8,128)(2,1)}, bf16[96,2,1536]{2,0,1:T(8,128)(2,1)S(1)}, u32[]{:S(2)}, u32[]{:S(2)}) collective-permute-start(bf16[96,2,1536]{2,0,1:T(8,128)(2,1)} %collective-permute-done.3), channel_id=1, source_target_pairs={{0,224},{32,0},{64,32},{96,64},{128,96},{160,128},{192,160},{224,1... | collective-permute-start | bytes 1769480 | tf_op jit(solution)/shard_map/ppermute | solution.py:83
  206.2 10.5 %collective-permute-start.6 = (bf16[96,2,1536]{2,0,1:T(8,128)(2,1)S(1)}, bf16[96,2,1536]{2,0,1:T(8,128)(2,1)S(1)}, u32[]{:S(2)}, u32[]{:S(2)}) collective-permute-start(bf16[96,2,1536]{2,0,1:T(8,128)(2,1)S(1)} %collective-permute-done.4), channel_id=1, source_target_pairs={{0,32},{32,64},{64,96},{96,128},{128,160},{160,192},{192,224},{224... | collective-permute-start | bytes 1769480 | tf_op jit(solution)/shard_map/ppermute | solution.py:78
  223.9 41.9 %all-to-all-start.2 = ((bf16[2,32,24,512]{3,2,0,1:T(8,128)(2,1)}), bf16[2,32,24,512]{3,2,0,1:T(8,128)(2,1)S(1)}, u32[]{:S(2)}, u32[]{:S(2)}) async-start(bf16[2,32,24,512]{3,2,0,1:T(8,128)(2,1)} %copy.68), calls=%async_computation.3 | async-start | bytes 3145728 | tf_op jit(solution)/shard_map/all_to_all | solution.py:115
  265.8 37.2 %all-to-all-start.1 = ((bf16[2,32,24,512]{3,2,0,1:T(8,128)(2,1)}), bf16[2,32,24,512]{3,2,0,1:T(8,128)(2,1)S(1)}, u32[]{:S(2)}, u32[]{:S(2)}) async-start(bf16[2,32,24,512]{3,2,0,1:T(8,128)(2,1)} %copy.66), calls=%async_computation.2 | async-start | bytes 3145728 | tf_op jit(solution)/shard_map/all_to_all | solution.py:91
  272.1 7.3 %copy-start.4 = (bf16[1,2,32,24,512]{4,3,2,1,0:T(8,128)(2,1)S(1)}, bf16[1,2,32,24,512]{4,3,2,1,0:T(8,128)(2,1)}, u32[]{:S(2)}) copy-start(bf16[1,2,32,24,512]{4,3,2,1,0:T(8,128)(2,1)} %copy-done.3) | copy-start | bytes 4718596
  272.1 7.3 %copy-start.7 = (bf16[768,2,768]{2,0,1:T(8,128)(2,1)S(1)}, bf16[768,2,768]{2,0,1:T(8,128)(2,1)}, u32[]{:S(2)}) copy-start(bf16[768,2,768]{2,0,1:T(8,128)(2,1)} %all-gather.2.cloned.1.call-done) | copy-start | bytes 7077892
  303.1 2.9 copy-start.5
  303.1 37.8 %copy-start.1 = (bf16[2,512,1536]{2,1,0:T(8,128)(2,1)S(1)}, bf16[2,512,1536]{2,1,0:T(8,128)(2,1)}, u32[]{:S(2)}) copy-start(bf16[2,512,1536]{2,1,0:T(8,128)(2,1)} %param.9) | copy-start | bytes 9437188
Sparse Core Ops, SparseCore 0:
  115.5 45.7 reduce-scatter.1
  180.6 29.4 all-gather.1
